TPU v7x, 32 devices: a whole 2x2x4 slice. The times are simulated.
32 devices in a mesh: tm: 8 (over y, x, core), space: 4 (over z).
Axes of the slice: x: 2, y: 2, z: 4, core: 2. Of those that a mesh axis runs over, the one named last changes fastest.
Arguments:
- starts: float32 [8, 32, 128, 128], P('tm', 'space'), may hold values from -6 to 6
- diffusivity: float32 [32, 128, 128], P('space'), may hold values from 0.04 to 0.2
- velocity: float32 [2, 32, 128, 128], P(None, 'space'), may hold values from -0.1 to 0.1
- obstacle: int32 [32, 128, 128], P('space'), may hold values from 0 to 1, as said below
- substep_scale: float32 [12], replicated, may hold values from 0.5 to 1
- neighbors: int32 [32, 4], P('space'), may hold values from 0 to 32, as said below
- coarse_x: float32 [32, 64, 64], P('space'), may hold values from -1 to 1
- coarse_y: float32 [32, 128, 128], P('space'), may hold values from -1 to 1
Outputs:
- slice_ends: float32 [8, 32, 128, 128], P('tm', 'space')
- increment: float32 [8, 32, 128, 128], P('tm', 'space')
Inputs may be any that keep to these rules, and one draw needn't show every extreme that they name: `neighbors`: tiles form a grid of 4 by 8; each entry names the tile beside a tile in the given direction, or 32 on the grid's edge. The tiles 8 * k to 8 * (k + 1) - 1 fill grid row k, in any order within it, so a neighbour's number differs from the tile's block k by at most one block. `obstacle`: each tile holds one tube, a disc of radius 128 // 8 to 32 cells.
All inputs are finite; a program needn't handle non-finite values.
Results may differ from a plain program's by a relative error of at most 0.0002.
Values sent between devices are 32-bit elements; how exact they have to be, the bound alone decides.
No kernel may reach another device: no remote copies, remote signals or barrier semaphores. Data moves between devices by JAX's collectives and lax.ppermute only.
A program may use at most 128 MiB of HBM per device.

v0:
```python
import jax
import jax.numpy as jnp
from jax import lax
from jax.sharding import PartitionSpec as P

SUB = 12
exact_precision = lax.Precision.HIGHEST


def padded(block, sides, width):
    for axis, dim in sides:
        count = lax.axis_size(axis)
        forward = [(i, i + 1) for i in range(count - 1)]
        backward = [(target, source) for source, target in forward]
        low = lax.ppermute(
            lax.slice_in_dim(block, block.shape[dim] - width, None, axis=dim), axis, forward
        )
        high = lax.ppermute(lax.slice_in_dim(block, 0, width, axis=dim), axis, backward)
        block = jnp.concatenate([low, block, high], axis=dim)
    return block


def spread(value, axis, source):
    kept = jnp.where(lax.axis_index(axis) == source, value, 0).astype(value.dtype)
    return lax.psum(kept, axis)


def passed_along(block, axis, distance):
    devices = range(lax.axis_size(axis))
    route = [(i - distance, i) for i in devices if i - distance in devices]
    return lax.ppermute(block, axis, route)


def restrict(values):
    return 0.5 * (values[..., 0::2, :] + values[..., 1::2, :])


def prolong(coarse_values):
    return jnp.repeat(coarse_values, 2, axis=-2)


def apply_coarse(coarse_values, matrix_x, matrix_y):
    mixed_x = jnp.einsum("tij,...tjk->...tik", matrix_x, coarse_values, precision=exact_precision)
    return jnp.einsum("...tik,tlk->...til", mixed_x, matrix_y, precision=exact_precision)


def on_device(
    starts, diffusivity, velocity, obstacle, substep_scale, neighbors, coarse_x, coarse_y
):
    slice_count = starts.shape[0]
    tile_count = starts.shape[1]
    all_tiles = tile_count * lax.axis_size("space")
    block_base = lax.axis_index("space") * tile_count
    open_cells = 1.0 - obstacle.astype(jnp.float32)
    speed_x = velocity[0]
    speed_y = velocity[1]
    shifted = neighbors - block_base + tile_count
    lookup_index = jnp.where(neighbors == all_tiles, 3 * tile_count, shifted)

    def advance(substep_index, current):
        strength = substep_scale[substep_index]
        own_faces = jnp.stack(
            [current[:, :, 0, :], current[:, :, -1, :], current[:, :, :, 0], current[:, :, :, -1]],
            axis=2,
        )
        gathered = padded(own_faces, (("space", 1),), tile_count)
        gathered = jnp.concatenate([gathered, jnp.zeros_like(gathered[:, :1])], axis=1)
        west_face = gathered[:, lookup_index[:, 0], 1]
        east_face = gathered[:, lookup_index[:, 1], 0]
        south_face = gathered[:, lookup_index[:, 2], 3]
        north_face = gathered[:, lookup_index[:, 3], 2]
        from_west = jnp.concatenate([west_face[:, :, None, :], current[:, :, :-1, :]], axis=2)
        from_east = jnp.concatenate([current[:, :, 1:, :], east_face[:, :, None, :]], axis=2)
        from_south = jnp.concatenate([south_face[:, :, :, None], current[:, :, :, :-1]], axis=3)
        from_north = jnp.concatenate([current[:, :, :, 1:], north_face[:, :, :, None]], axis=3)
        laplace = from_west + from_east + from_south + from_north - 4.0 * current
        transport = speed_x * (from_east - from_west) + speed_y * (from_north - from_south)
        return open_cells * (current + strength * diffusivity * laplace - 0.5 * transport)

    fine_ends = lax.fori_loop(0, SUB, advance, starts)
    correction = fine_ends - prolong(apply_coarse(restrict(starts), coarse_x, coarse_y))
    coarse_jump = restrict(correction)
    first_coarse = spread(restrict(starts[0]), "tm", 0)
    every_jump = lax.all_gather(coarse_jump, "tm", axis=0, tiled=True)

    def sweep(state_now, jump):
        return (apply_coarse(state_now, coarse_x, coarse_y) + jump, state_now)

    last_state, history = lax.scan(sweep, first_coarse, every_jump)
    own_coarse = lax.dynamic_slice_in_dim(
        history, lax.axis_index("tm") * slice_count, slice_count, 0
    )
    slice_ends = prolong(apply_coarse(own_coarse, coarse_x, coarse_y)) + correction
    previous = passed_along(slice_ends[-1], "tm", 1)
    first_step = jnp.where(
        lax.axis_index("tm") == 0, jnp.zeros_like(previous), previous - starts[0]
    )
    increment = jnp.concatenate([first_step[None], slice_ends[:-1] - starts[1:]], axis=0)
    return (slice_ends, increment)


def solution(mesh):
    placed = (
        P("tm", "space", None, None),
        P("space", None, None),
        P(None, "space", None, None),
        P("space", None, None),
        P(),
        P("space", None),
        P("space", None, None),
        P("space", None, None),
    )
    return jax.shard_map(
        on_device,
        mesh=mesh,
        in_specs=placed,
        out_specs=(P("tm", "space", None, None), P("tm", "space", None, None)),
        check_vma=False,
    )
```

profile of v0, /device:TPU:4, one launch (start us, length us, event | category | flops | bytes accessed | tf_op | source)
XLA Modules:
  0.0 285.6 jit_solution(6165159158150083791)
XLA Ops:
  16.3 170.8 %while.25 = (s32[]{:T(128)}, f32[1,8,128,128]{2,1,3,0:T(8,128)S(1)}, f32[8,128,128]{1,0,2:T(8,128)}, f32[12]{0:T(128)S(1)}, f32[8,128,128]{1,0,2:T(8,128)}, /*in...) while((s32[]{:T(128)}, ...), condition=%wide.region_2.3_spmd, body=%wide.region_1.2_spmd.sunk | while | flops 2710714 | bytes 10800037 | solution.py:80
  16.6 3.5 %collective-permute-start.1 = (f32[1,8,4,128]{3,2,1,0:T(4,128)S(1)}, f32[1,8,4,128]{3,2,1,0:T(4,128)S(1)}, u32[]{:S(2)}, u32[]{:S(2)}) collective-permute-start(f32[1,8,4,128]{3,2,1,0:T(4,128)S(1)} %pad_maximum_fusion.6), channel_id=1, source_target_pairs={{0,1},{1,2},{2,3},{4,5},{5,6},{6,7},{8,9},{9,10},{10,11},{12,13},{... | collective-permute-start | bytes 49160 | tf_op jit(solution)/shard_map/while/body/eval_jaxpr/ppermute | solution.py:15
  23.1 2.6 collective-permute-done
  28.7 3.0 %fusion.60 = f32[1,8,128,128]{2,1,3,0:T(8,128)S(1)} fusion(f32[1,8,128,128]{2,1,3,0:T(8,128)S(1)} %get-tuple-element.355, f32[8,128,128]{1,0,2:T(8,128)} %get-tuple-element.367, f32[1,8,128,128]{2,1,3,0:T(8,128)} %get-tuple-element.372, f32[1,8,128,128]{2,1,3,0:T(8,128)} %get-tuple-element.371, f32[1,8,128,1]{2,1,3,0:T(8,128)S(1)} %bitcast.113, ...), kind=kLoop, calls=%fused_computation.13.clone.1 | loop fusion | flops 2621440 | bytes 5242884 | tf_op jit(solution)/shard_map/while/body/eval_jaxpr/mul | solution.py:78
  31.9 3.5 %collective-permute-start.1 = (f32[1,8,4,128]{3,2,1,0:T(4,128)S(1)}, f32[1,8,4,128]{3,2,1,0:T(4,128)S(1)}, u32[]{:S(2)}, u32[]{:S(2)}) collective-permute-start(f32[1,8,4,128]{3,2,1,0:T(4,128)S(1)} %pad_maximum_fusion.6), channel_id=1, source_target_pairs={{0,1},{1,2},{2,3},{4,5},{5,6},{6,7},{8,9},{9,10},{10,11},{12,13},{... | collective-permute-start | bytes 49160 | tf_op jit(solution)/shard_map/while/body/eval_jaxpr/ppermute | solution.py:15
  38.5 2.6 collective-permute-done
  44.0 3.0 %fusion.60 = f32[1,8,128,128]{2,1,3,0:T(8,128)S(1)} fusion(f32[1,8,128,128]{2,1,3,0:T(8,128)S(1)} %get-tuple-element.355, f32[8,128,128]{1,0,2:T(8,128)} %get-tuple-element.367, f32[1,8,128,128]{2,1,3,0:T(8,128)} %get-tuple-element.372, f32[1,8,128,128]{2,1,3,0:T(8,128)} %get-tuple-element.371, f32[1,8,128,1]{2,1,3,0:T(8,128)S(1)} %bitcast.113, ...), kind=kLoop, calls=%fused_computation.13.clone.1 | loop fusion | flops 2621440 | bytes 5242884 | tf_op jit(solution)/shard_map/while/body/eval_jaxpr/mul | solution.py:78
  47.3 3.5 %collective-permute-start.1 = (f32[1,8,4,128]{3,2,1,0:T(4,128)S(1)}, f32[1,8,4,128]{3,2,1,0:T(4,128)S(1)}, u32[]{:S(2)}, u32[]{:S(2)}) collective-permute-start(f32[1,8,4,128]{3,2,1,0:T(4,128)S(1)} %pad_maximum_fusion.6), channel_id=1, source_target_pairs={{0,1},{1,2},{2,3},{4,5},{5,6},{6,7},{8,9},{9,10},{10,11},{12,13},{... | collective-permute-start | bytes 49160 | tf_op jit(solution)/shard_map/while/body/eval_jaxpr/ppermute | solution.py:15
  53.9 2.6 collective-permute-done
  59.4 3.0 %fusion.60 = f32[1,8,128,128]{2,1,3,0:T(8,128)S(1)} fusion(f32[1,8,128,128]{2,1,3,0:T(8,128)S(1)} %get-tuple-element.355, f32[8,128,128]{1,0,2:T(8,128)} %get-tuple-element.367, f32[1,8,128,128]{2,1,3,0:T(8,128)} %get-tuple-element.372, f32[1,8,128,128]{2,1,3,0:T(8,128)} %get-tuple-element.371, f32[1,8,128,1]{2,1,3,0:T(8,128)S(1)} %bitcast.113, ...), kind=kLoop, calls=%fused_computation.13.clone.1 | loop fusion | flops 2621440 | bytes 5242884 | tf_op jit(solution)/shard_map/while/body/eval_jaxpr/mul | solution.py:78
  62.7 2.0 collective-permute-start.1
  67.7 2.6 collective-permute-done
  73.3 3.0 %fusion.60 = f32[1,8,128,128]{2,1,3,0:T(8,128)S(1)} fusion(f32[1,8,128,128]{2,1,3,0:T(8,128)S(1)} %get-tuple-element.355, f32[8,128,128]{1,0,2:T(8,128)} %get-tuple-element.367, f32[1,8,128,128]{2,1,3,0:T(8,128)} %get-tuple-element.372, f32[1,8,128,128]{2,1,3,0:T(8,128)} %get-tuple-element.371, f32[1,8,128,1]{2,1,3,0:T(8,128)S(1)} %bitcast.113, ...), kind=kLoop, calls=%fused_computation.13.clone.1 | loop fusion | flops 2621440 | bytes 5242884 | tf_op jit(solution)/shard_map/while/body/eval_jaxpr/mul | solution.py:78
  76.5 2.0 collective-permute-start.1
  81.6 2.6 collective-permute-done
  87.1 3.0 %fusion.60 = f32[1,8,128,128]{2,1,3,0:T(8,128)S(1)} fusion(f32[1,8,128,128]{2,1,3,0:T(8,128)S(1)} %get-tuple-element.355, f32[8,128,128]{1,0,2:T(8,128)} %get-tuple-element.367, f32[1,8,128,128]{2,1,3,0:T(8,128)} %get-tuple-element.372, f32[1,8,128,128]{2,1,3,0:T(8,128)} %get-tuple-element.371, f32[1,8,128,1]{2,1,3,0:T(8,128)S(1)} %bitcast.113, ...), kind=kLoop, calls=%fused_computation.13.clone.1 | loop fusion | flops 2621440 | bytes 5242884 | tf_op jit(solution)/shard_map/while/body/eval_jaxpr/mul | solution.py:78
  90.4 2.0 collective-permute-start.1
  95.5 2.6 collective-permute-done
  101.0 3.0 %fusion.60 = f32[1,8,128,128]{2,1,3,0:T(8,128)S(1)} fusion(f32[1,8,128,128]{2,1,3,0:T(8,128)S(1)} %get-tuple-element.355, f32[8,128,128]{1,0,2:T(8,128)} %get-tuple-element.367, f32[1,8,128,128]{2,1,3,0:T(8,128)} %get-tuple-element.372, f32[1,8,128,128]{2,1,3,0:T(8,128)} %get-tuple-element.371, f32[1,8,128,1]{2,1,3,0:T(8,128)S(1)} %bitcast.113, ...), kind=kLoop, calls=%fused_computation.13.clone.1 | loop fusion | flops 2621440 | bytes 5242884 | tf_op jit(solution)/shard_map/while/body/eval_jaxpr/mul | solution.py:78
  104.3 2.0 collective-permute-start.1
  109.3 2.6 collective-permute-done
  114.9 3.0 %fusion.60 = f32[1,8,128,128]{2,1,3,0:T(8,128)S(1)} fusion(f32[1,8,128,128]{2,1,3,0:T(8,128)S(1)} %get-tuple-element.355, f32[8,128,128]{1,0,2:T(8,128)} %get-tuple-element.367, f32[1,8,128,128]{2,1,3,0:T(8,128)} %get-tuple-element.372, f32[1,8,128,128]{2,1,3,0:T(8,128)} %get-tuple-element.371, f32[1,8,128,1]{2,1,3,0:T(8,128)S(1)} %bitcast.113, ...), kind=kLoop, calls=%fused_computation.13.clone.1 | loop fusion | flops 2621440 | bytes 5242884 | tf_op jit(solution)/shard_map/while/body/eval_jaxpr/mul | solution.py:78
  118.1 2.0 collective-permute-start.1
  123.2 2.6 collective-permute-done
  128.7 3.0 %fusion.60 = f32[1,8,128,128]{2,1,3,0:T(8,128)S(1)} fusion(f32[1,8,128,128]{2,1,3,0:T(8,128)S(1)} %get-tuple-element.355, f32[8,128,128]{1,0,2:T(8,128)} %get-tuple-element.367, f32[1,8,128,128]{2,1,3,0:T(8,128)} %get-tuple-element.372, f32[1,8,128,128]{2,1,3,0:T(8,128)} %get-tuple-element.371, f32[1,8,128,1]{2,1,3,0:T(8,128)S(1)} %bitcast.113, ...), kind=kLoop, calls=%fused_computation.13.clone.1 | loop fusion | flops 2621440 | bytes 5242884 | tf_op jit(solution)/shard_map/while/body/eval_jaxpr/mul | solution.py:78
  132.0 2.0 collective-permute-start.1
  137.0 2.6 collective-permute-done
  142.6 3.0 %fusion.60 = f32[1,8,128,128]{2,1,3,0:T(8,128)S(1)} fusion(f32[1,8,128,128]{2,1,3,0:T(8,128)S(1)} %get-tuple-element.355, f32[8,128,128]{1,0,2:T(8,128)} %get-tuple-element.367, f32[1,8,128,128]{2,1,3,0:T(8,128)} %get-tuple-element.372, f32[1,8,128,128]{2,1,3,0:T(8,128)} %get-tuple-element.371, f32[1,8,128,1]{2,1,3,0:T(8,128)S(1)} %bitcast.113, ...), kind=kLoop, calls=%fused_computation.13.clone.1 | loop fusion | flops 2621440 | bytes 5242884 | tf_op jit(solution)/shard_map/while/body/eval_jaxpr/mul | solution.py:78
  145.8 2.0 collective-permute-start.1
  150.9 2.6 collective-permute-done
  156.4 3.0 %fusion.60 = f32[1,8,128,128]{2,1,3,0:T(8,128)S(1)} fusion(f32[1,8,128,128]{2,1,3,0:T(8,128)S(1)} %get-tuple-element.355, f32[8,128,128]{1,0,2:T(8,128)} %get-tuple-element.367, f32[1,8,128,128]{2,1,3,0:T(8,128)} %get-tuple-element.372, f32[1,8,128,128]{2,1,3,0:T(8,128)} %get-tuple-element.371, f32[1,8,128,1]{2,1,3,0:T(8,128)S(1)} %bitcast.113, ...), kind=kLoop, calls=%fused_computation.13.clone.1 | loop fusion | flops 2621440 | bytes 5242884 | tf_op jit(solution)/shard_map/while/body/eval_jaxpr/mul | solution.py:78
  159.7 2.0 collective-permute-start.1
  164.8 2.6 collective-permute-done
  170.3 3.0 %fusion.60 = f32[1,8,128,128]{2,1,3,0:T(8,128)S(1)} fusion(f32[1,8,128,128]{2,1,3,0:T(8,128)S(1)} %get-tuple-element.355, f32[8,128,128]{1,0,2:T(8,128)} %get-tuple-element.367, f32[1,8,128,128]{2,1,3,0:T(8,128)} %get-tuple-element.372, f32[1,8,128,128]{2,1,3,0:T(8,128)} %get-tuple-element.371, f32[1,8,128,1]{2,1,3,0:T(8,128)S(1)} %bitcast.113, ...), kind=kLoop, calls=%fused_computation.13.clone.1 | loop fusion | flops 2621440 | bytes 5242884 | tf_op jit(solution)/shard_map/while/body/eval_jaxpr/mul | solution.py:78
  173.6 2.0 collective-permute-start.1
  178.6 2.6 collective-permute-done
  184.2 3.0 %fusion.60 = f32[1,8,128,128]{2,1,3,0:T(8,128)S(1)} fusion(f32[1,8,128,128]{2,1,3,0:T(8,128)S(1)} %get-tuple-element.355, f32[8,128,128]{1,0,2:T(8,128)} %get-tuple-element.367, f32[1,8,128,128]{2,1,3,0:T(8,128)} %get-tuple-element.372, f32[1,8,128,128]{2,1,3,0:T(8,128)} %get-tuple-element.371, f32[1,8,128,1]{2,1,3,0:T(8,128)S(1)} %bitcast.113, ...), kind=kLoop, calls=%fused_computation.13.clone.1 | loop fusion | flops 2621440 | bytes 5242884 | tf_op jit(solution)/shard_map/while/body/eval_jaxpr/mul | solution.py:78
  187.4 1.4 convolution_bitcast_fusion.1
  191.3 26.0 %all-gather.2.cloned.1.call-done = f32[8,8,64,128]{3,2,1,0:T(8,128)} async-done(((f32[1,8,64,128]{3,2,1,0:T(8,128)}), f32[8,8,64,128]{3,2,1,0:T(8,128)}) %all-gather.2.cloned.1.call-update) | async-done | bytes 2097168 | tf_op jit(solution)/shard_map/all_gather | solution.py:84
  217.2 46.5 %while.26 = (s32[]{:T(128)}, f32[8,64,128]{2,1,0:T(8,128)}, f32[8,8,64,128]{3,2,1,0:T(8,128)}, f32[8,64,64]{2,1,0:T(8,128)S(1)}, f32[8,128,128]{2,1,0:T(8,128)S(1)}, /*index=5*/f32[8,8,64,128]{3,2,1,0:T(8,128)}, s32[]{:T(128)}) while((s32[]{:T(128)}, f32[8,64,128]{2,1,0:T(8,128)}, f32[8,8,64,128]{3,2,1,0:T(8,128)}, ...), condition=%wide.region_4.5_spmd, body=%wide.region_3.4_spmd.sunk | while | flops 151060480 | bytes 2490461 | solution.py:89
  217.2 1.3 fusion.65
  218.6 1.7 bitcast_dynamic-update-slice_fusion.2
  220.3 2.8 convolution_add_fusion.2
  223.0 1.3 fusion.65
  224.4 1.7 bitcast_dynamic-update-slice_fusion.2
  226.1 2.8 convolution_add_fusion.2
  228.9 1.3 fusion.65
  230.2 1.7 bitcast_dynamic-update-slice_fusion.2
  231.9 2.8 convolution_add_fusion.2
  234.7 1.3 fusion.65
  236.0 1.7 bitcast_dynamic-update-slice_fusion.2
  237.7 2.8 convolution_add_fusion.2
  240.5 1.3 fusion.65
  241.8 1.7 bitcast_dynamic-update-slice_fusion.2
  243.5 2.8 convolution_add_fusion.2
  247.6 1.7 bitcast_dynamic-update-slice_fusion.2
  249.3 2.8 convolution_add_fusion.2
  253.4 1.7 bitcast_dynamic-update-slice_fusion.2
  255.1 2.8 convolution_add_fusion.2
  259.2 1.7 bitcast_dynamic-update-slice_fusion.2
  260.9 2.8 convolution_add_fusion.2
  263.7 1.4 convolution_bitcast_fusion
  266.5 2.1 collective-permute-start.2
  268.6 9.3 %collective-permute-done.2 = f32[8,128,128]{2,1,0:T(8,128)S(1)} collective-permute-done((f32[8,128,128]{2,1,0:T(8,128)S(1)}, f32[8,128,128]{2,1,0:T(8,128)S(1)}, u32[]{:S(2)}, u32[]{:S(2)}) %collective-permute-start.2) | collective-permute-done | bytes 524320 | tf_op jit(solution)/shard_map/ppermute | solution.py:31
  (269 shorter events, 92.7 us)
Async XLA Ops:
  7.2 3.1 %copy-start.2 = (f32[1,8,128,128]{3,2,1,0:T(8,128)S(1)}, f32[1,8,128,128]{3,2,1,0:T(8,128)}, u32[]{:S(2)}) copy-start(f32[1,8,128,128]{3,2,1,0:T(8,128)} %param.12) | copy-start | bytes 1572868
  7.2 184.1 %all-reduce.6.cloned.1.call-start = ((), (), s32[]{:S(2)}) async-start(), calls=%async_computation | async-start | bytes 524288 | tf_op jit(solution)/shard_map/psum | solution.py:25
  7.2 4.8 %copy-start.6 = (f32[8,128,128]{2,1,0:T(8,128)S(1)}, f32[8,128,128]{2,1,0:T(8,128)}, u32[]{:S(2)}) copy-start(f32[8,128,128]{2,1,0:T(8,128)} %param.13) | copy-start | bytes 1572868
  9.4 3.6 %copy-start.7 = (s32[8,128,128]{2,1,0:T(8,128)S(1)}, s32[8,128,128]{2,1,0:T(8,128)}, u32[]{:S(2)}) copy-start(s32[8,128,128]{2,1,0:T(8,128)} %param.15) | copy-start | bytes 1572868
  10.2 207.0 %all-gather.2.cloned.1.call-start = ((), (), s32[]{:S(2)}) async-start(), calls=%async_computation.1 | async-start | bytes 2359296 | tf_op jit(solution)/shard_map/all_gather | solution.py:84
  11.8 2.3 copy-start.4
  14.1 2.1 copy-start.8
  14.1 2.1 copy-start.9
  16.3 171.1 %copy-start.1 = (f32[8,64,64]{2,1,0:T(8,128)S(1)}, f32[8,64,64]{2,1,0:T(8,128)}, u32[]{:S(2)}) copy-start(f32[8,64,64]{2,1,0:T(8,128)} %param.18) | copy-start | bytes 393220
  16.6 6.6 %collective-permute-start.1 = (f32[1,8,4,128]{3,2,1,0:T(4,128)S(1)}, f32[1,8,4,128]{3,2,1,0:T(4,128)S(1)}, u32[]{:S(2)}, u32[]{:S(2)}) collective-permute-start(f32[1,8,4,128]{3,2,1,0:T(4,128)S(1)} %pad_maximum_fusion.6), channel_id=1, source_target_pairs={{0,1},{1,2},{2,3},{4,5},{5,6},{6,7},{8,9},{9,10},{10,11},{12,13},{... | collective-permute-start | bytes 49160 | tf_op jit(solution)/shard_map/while/body/eval_jaxpr/ppermute | solution.py:15
  20.1 5.6 %collective-permute-start = (f32[1,8,4,128]{3,2,1,0:T(4,128)S(1)}, f32[1,8,4,128]{3,2,1,0:T(4,128)S(1)}, u32[]{:S(2)}, u32[]{:S(2)}) collective-permute-start(f32[1,8,4,128]{3,2,1,0:T(4,128)S(1)} %pad_maximum_fusion.6), channel_id=1, source_target_pairs={{1,0},{2,1},{3,2},{5,4},{6,5},{7,6},{9,8},{10,9},{11,10},{13,12},{... | collective-permute-start | bytes 49160 | tf_op jit(solution)/shard_map/while/body/eval_jaxpr/ppermute | solution.py:18
  31.9 6.6 %collective-permute-start.1 = (f32[1,8,4,128]{3,2,1,0:T(4,128)S(1)}, f32[1,8,4,128]{3,2,1,0:T(4,128)S(1)}, u32[]{:S(2)}, u32[]{:S(2)}) collective-permute-start(f32[1,8,4,128]{3,2,1,0:T(4,128)S(1)} %pad_maximum_fusion.6), channel_id=1, source_target_pairs={{0,1},{1,2},{2,3},{4,5},{5,6},{6,7},{8,9},{9,10},{10,11},{12,13},{... | collective-permute-start | bytes 49160 | tf_op jit(solution)/shard_map/while/body/eval_jaxpr/ppermute | solution.py:15
  35.4 5.6 %collective-permute-start = (f32[1,8,4,128]{3,2,1,0:T(4,128)S(1)}, f32[1,8,4,128]{3,2,1,0:T(4,128)S(1)}, u32[]{:S(2)}, u32[]{:S(2)}) collective-permute-start(f32[1,8,4,128]{3,2,1,0:T(4,128)S(1)} %pad_maximum_fusion.6), channel_id=1, source_target_pairs={{1,0},{2,1},{3,2},{5,4},{6,5},{7,6},{9,8},{10,9},{11,10},{13,12},{... | collective-permute-start | bytes 49160 | tf_op jit(solution)/shard_map/while/body/eval_jaxpr/ppermute | solution.py:18
  47.3 6.6 %collective-permute-start.1 = (f32[1,8,4,128]{3,2,1,0:T(4,128)S(1)}, f32[1,8,4,128]{3,2,1,0:T(4,128)S(1)}, u32[]{:S(2)}, u32[]{:S(2)}) collective-permute-start(f32[1,8,4,128]{3,2,1,0:T(4,128)S(1)} %pad_maximum_fusion.6), channel_id=1, source_target_pairs={{0,1},{1,2},{2,3},{4,5},{5,6},{6,7},{8,9},{9,10},{10,11},{12,13},{... | collective-permute-start | bytes 49160 | tf_op jit(solution)/shard_map/while/body/eval_jaxpr/ppermute | solution.py:15
  50.8 5.6 %collective-permute-start = (f32[1,8,4,128]{3,2,1,0:T(4,128)S(1)}, f32[1,8,4,128]{3,2,1,0:T(4,128)S(1)}, u32[]{:S(2)}, u32[]{:S(2)}) collective-permute-start(f32[1,8,4,128]{3,2,1,0:T(4,128)S(1)} %pad_maximum_fusion.6), channel_id=1, source_target_pairs={{1,0},{2,1},{3,2},{5,4},{6,5},{7,6},{9,8},{10,9},{11,10},{13,12},{... | collective-permute-start | bytes 49160 | tf_op jit(solution)/shard_map/while/body/eval_jaxpr/ppermute | solution.py:18
  62.7 5.1 %collective-permute-start.1 = (f32[1,8,4,128]{3,2,1,0:T(4,128)S(1)}, f32[1,8,4,128]{3,2,1,0:T(4,128)S(1)}, u32[]{:S(2)}, u32[]{:S(2)}) collective-permute-start(f32[1,8,4,128]{3,2,1,0:T(4,128)S(1)} %pad_maximum_fusion.6), channel_id=1, source_target_pairs={{0,1},{1,2},{2,3},{4,5},{5,6},{6,7},{8,9},{9,10},{10,11},{12,13},{... | collective-permute-start | bytes 49160 | tf_op jit(solution)/shard_map/while/body/eval_jaxpr/ppermute | solution.py:15
  64.7 5.6 %collective-permute-start = (f32[1,8,4,128]{3,2,1,0:T(4,128)S(1)}, f32[1,8,4,128]{3,2,1,0:T(4,128)S(1)}, u32[]{:S(2)}, u32[]{:S(2)}) collective-permute-start(f32[1,8,4,128]{3,2,1,0:T(4,128)S(1)} %pad_maximum_fusion.6), channel_id=1, source_target_pairs={{1,0},{2,1},{3,2},{5,4},{6,5},{7,6},{9,8},{10,9},{11,10},{13,12},{... | collective-permute-start | bytes 49160 | tf_op jit(solution)/shard_map/while/body/eval_jaxpr/ppermute | solution.py:18
  76.5 5.1 %collective-permute-start.1 = (f32[1,8,4,128]{3,2,1,0:T(4,128)S(1)}, f32[1,8,4,128]{3,2,1,0:T(4,128)S(1)}, u32[]{:S(2)}, u32[]{:S(2)}) collective-permute-start(f32[1,8,4,128]{3,2,1,0:T(4,128)S(1)} %pad_maximum_fusion.6), channel_id=1, source_target_pairs={{0,1},{1,2},{2,3},{4,5},{5,6},{6,7},{8,9},{9,10},{10,11},{12,13},{... | collective-permute-start | bytes 49160 | tf_op jit(solution)/shard_map/while/body/eval_jaxpr/ppermute | solution.py:15
  78.5 5.6 %collective-permute-start = (f32[1,8,4,128]{3,2,1,0:T(4,128)S(1)}, f32[1,8,4,128]{3,2,1,0:T(4,128)S(1)}, u32[]{:S(2)}, u32[]{:S(2)}) collective-permute-start(f32[1,8,4,128]{3,2,1,0:T(4,128)S(1)} %pad_maximum_fusion.6), channel_id=1, source_target_pairs={{1,0},{2,1},{3,2},{5,4},{6,5},{7,6},{9,8},{10,9},{11,10},{13,12},{... | collective-permute-start | bytes 49160 | tf_op jit(solution)/shard_map/while/body/eval_jaxpr/ppermute | solution.py:18
  90.4 5.1 %collective-permute-start.1 = (f32[1,8,4,128]{3,2,1,0:T(4,128)S(1)}, f32[1,8,4,128]{3,2,1,0:T(4,128)S(1)}, u32[]{:S(2)}, u32[]{:S(2)}) collective-permute-start(f32[1,8,4,128]{3,2,1,0:T(4,128)S(1)} %pad_maximum_fusion.6), channel_id=1, source_target_pairs={{0,1},{1,2},{2,3},{4,5},{5,6},{6,7},{8,9},{9,10},{10,11},{12,13},{... | collective-permute-start | bytes 49160 | tf_op jit(solution)/shard_map/while/body/eval_jaxpr/ppermute | solution.py:15
  92.4 5.6 %collective-permute-start = (f32[1,8,4,128]{3,2,1,0:T(4,128)S(1)}, f32[1,8,4,128]{3,2,1,0:T(4,128)S(1)}, u32[]{:S(2)}, u32[]{:S(2)}) collective-permute-start(f32[1,8,4,128]{3,2,1,0:T(4,128)S(1)} %pad_maximum_fusion.6), channel_id=1, source_target_pairs={{1,0},{2,1},{3,2},{5,4},{6,5},{7,6},{9,8},{10,9},{11,10},{13,12},{... | collective-permute-start | bytes 49160 | tf_op jit(solution)/shard_map/while/body/eval_jaxpr/ppermute | solution.py:18
  104.3 5.1 %collective-permute-start.1 = (f32[1,8,4,128]{3,2,1,0:T(4,128)S(1)}, f32[1,8,4,128]{3,2,1,0:T(4,128)S(1)}, u32[]{:S(2)}, u32[]{:S(2)}) collective-permute-start(f32[1,8,4,128]{3,2,1,0:T(4,128)S(1)} %pad_maximum_fusion.6), channel_id=1, source_target_pairs={{0,1},{1,2},{2,3},{4,5},{5,6},{6,7},{8,9},{9,10},{10,11},{12,13},{... | collective-permute-start | bytes 49160 | tf_op jit(solution)/shard_map/while/body/eval_jaxpr/ppermute | solution.py:15
  106.3 5.6 %collective-permute-start = (f32[1,8,4,128]{3,2,1,0:T(4,128)S(1)}, f32[1,8,4,128]{3,2,1,0:T(4,128)S(1)}, u32[]{:S(2)}, u32[]{:S(2)}) collective-permute-start(f32[1,8,4,128]{3,2,1,0:T(4,128)S(1)} %pad_maximum_fusion.6), channel_id=1, source_target_pairs={{1,0},{2,1},{3,2},{5,4},{6,5},{7,6},{9,8},{10,9},{11,10},{13,12},{... | collective-permute-start | bytes 49160 | tf_op jit(solution)/shard_map/while/body/eval_jaxpr/ppermute | solution.py:18
  118.1 5.1 %collective-permute-start.1 = (f32[1,8,4,128]{3,2,1,0:T(4,128)S(1)}, f32[1,8,4,128]{3,2,1,0:T(4,128)S(1)}, u32[]{:S(2)}, u32[]{:S(2)}) collective-permute-start(f32[1,8,4,128]{3,2,1,0:T(4,128)S(1)} %pad_maximum_fusion.6), channel_id=1, source_target_pairs={{0,1},{1,2},{2,3},{4,5},{5,6},{6,7},{8,9},{9,10},{10,11},{12,13},{... | collective-permute-start | bytes 49160 | tf_op jit(solution)/shard_map/while/body/eval_jaxpr/ppermute | solution.py:15
  120.1 5.6 %collective-permute-start = (f32[1,8,4,128]{3,2,1,0:T(4,128)S(1)}, f32[1,8,4,128]{3,2,1,0:T(4,128)S(1)}, u32[]{:S(2)}, u32[]{:S(2)}) collective-permute-start(f32[1,8,4,128]{3,2,1,0:T(4,128)S(1)} %pad_maximum_fusion.6), channel_id=1, source_target_pairs={{1,0},{2,1},{3,2},{5,4},{6,5},{7,6},{9,8},{10,9},{11,10},{13,12},{... | collective-permute-start | bytes 49160 | tf_op jit(solution)/shard_map/while/body/eval_jaxpr/ppermute | solution.py:18
  132.0 5.1 %collective-permute-start.1 = (f32[1,8,4,128]{3,2,1,0:T(4,128)S(1)}, f32[1,8,4,128]{3,2,1,0:T(4,128)S(1)}, u32[]{:S(2)}, u32[]{:S(2)}) collective-permute-start(f32[1,8,4,128]{3,2,1,0:T(4,128)S(1)} %pad_maximum_fusion.6), channel_id=1, source_target_pairs={{0,1},{1,2},{2,3},{4,5},{5,6},{6,7},{8,9},{9,10},{10,11},{12,13},{... | collective-permute-start | bytes 49160 | tf_op jit(solution)/shard_map/while/body/eval_jaxpr/ppermute | solution.py:15
  134.0 5.6 %collective-permute-start = (f32[1,8,4,128]{3,2,1,0:T(4,128)S(1)}, f32[1,8,4,128]{3,2,1,0:T(4,128)S(1)}, u32[]{:S(2)}, u32[]{:S(2)}) collective-permute-start(f32[1,8,4,128]{3,2,1,0:T(4,128)S(1)} %pad_maximum_fusion.6), channel_id=1, source_target_pairs={{1,0},{2,1},{3,2},{5,4},{6,5},{7,6},{9,8},{10,9},{11,10},{13,12},{... | collective-permute-start | bytes 49160 | tf_op jit(solution)/shard_map/while/body/eval_jaxpr/ppermute | solution.py:18
  145.8 5.1 %collective-permute-start.1 = (f32[1,8,4,128]{3,2,1,0:T(4,128)S(1)}, f32[1,8,4,128]{3,2,1,0:T(4,128)S(1)}, u32[]{:S(2)}, u32[]{:S(2)}) collective-permute-start(f32[1,8,4,128]{3,2,1,0:T(4,128)S(1)} %pad_maximum_fusion.6), channel_id=1, source_target_pairs={{0,1},{1,2},{2,3},{4,5},{5,6},{6,7},{8,9},{9,10},{10,11},{12,13},{... | collective-permute-start | bytes 49160 | tf_op jit(solution)/shard_map/while/body/eval_jaxpr/ppermute | solution.py:15
  147.8 5.6 %collective-permute-start = (f32[1,8,4,128]{3,2,1,0:T(4,128)S(1)}, f32[1,8,4,128]{3,2,1,0:T(4,128)S(1)}, u32[]{:S(2)}, u32[]{:S(2)}) collective-permute-start(f32[1,8,4,128]{3,2,1,0:T(4,128)S(1)} %pad_maximum_fusion.6), channel_id=1, source_target_pairs={{1,0},{2,1},{3,2},{5,4},{6,5},{7,6},{9,8},{10,9},{11,10},{13,12},{... | collective-permute-start | bytes 49160 | tf_op jit(solution)/shard_map/while/body/eval_jaxpr/ppermute | solution.py:18
  159.7 5.1 %collective-permute-start.1 = (f32[1,8,4,128]{3,2,1,0:T(4,128)S(1)}, f32[1,8,4,128]{3,2,1,0:T(4,128)S(1)}, u32[]{:S(2)}, u32[]{:S(2)}) collective-permute-start(f32[1,8,4,128]{3,2,1,0:T(4,128)S(1)} %pad_maximum_fusion.6), channel_id=1, source_target_pairs={{0,1},{1,2},{2,3},{4,5},{5,6},{6,7},{8,9},{9,10},{10,11},{12,13},{... | collective-permute-start | bytes 49160 | tf_op jit(solution)/shard_map/while/body/eval_jaxpr/ppermute | solution.py:15
  161.7 5.6 %collective-permute-start = (f32[1,8,4,128]{3,2,1,0:T(4,128)S(1)}, f32[1,8,4,128]{3,2,1,0:T(4,128)S(1)}, u32[]{:S(2)}, u32[]{:S(2)}) collective-permute-start(f32[1,8,4,128]{3,2,1,0:T(4,128)S(1)} %pad_maximum_fusion.6), channel_id=1, source_target_pairs={{1,0},{2,1},{3,2},{5,4},{6,5},{7,6},{9,8},{10,9},{11,10},{13,12},{... | collective-permute-start | bytes 49160 | tf_op jit(solution)/shard_map/while/body/eval_jaxpr/ppermute | solution.py:18
  173.6 5.1 %collective-permute-start.1 = (f32[1,8,4,128]{3,2,1,0:T(4,128)S(1)}, f32[1,8,4,128]{3,2,1,0:T(4,128)S(1)}, u32[]{:S(2)}, u32[]{:S(2)}) collective-permute-start(f32[1,8,4,128]{3,2,1,0:T(4,128)S(1)} %pad_maximum_fusion.6), channel_id=1, source_target_pairs={{0,1},{1,2},{2,3},{4,5},{5,6},{6,7},{8,9},{9,10},{10,11},{12,13},{... | collective-permute-start | bytes 49160 | tf_op jit(solution)/shard_map/while/body/eval_jaxpr/ppermute | solution.py:15
  175.6 5.6 %collective-permute-start = (f32[1,8,4,128]{3,2,1,0:T(4,128)S(1)}, f32[1,8,4,128]{3,2,1,0:T(4,128)S(1)}, u32[]{:S(2)}, u32[]{:S(2)}) collective-permute-start(f32[1,8,4,128]{3,2,1,0:T(4,128)S(1)} %pad_maximum_fusion.6), channel_id=1, source_target_pairs={{1,0},{2,1},{3,2},{5,4},{6,5},{7,6},{9,8},{10,9},{11,10},{13,12},{... | collective-permute-start | bytes 49160 | tf_op jit(solution)/shard_map/while/body/eval_jaxpr/ppermute | solution.py:18
  187.1 1.7 copy-start
  263.7 14.2 %copy-start.3 = (f32[1,8,128,128]{3,2,1,0:T(8,128)S(1)}, f32[1,8,128,128]{3,2,1,0:T(8,128)}, u32[]{:S(2)}) copy-start(f32[1,8,128,128]{3,2,1,0:T(8,128)} %param.12) | copy-start | bytes 1572868
  266.5 12.3 %copy-start.5 = (f32[1,8,128,128]{3,2,1,0:T(8,128)}, f32[1,8,128,128]{3,2,1,0:T(8,128)S(1)}, u32[]{:S(2)}) copy-start(f32[1,8,128,128]{3,2,1,0:T(8,128)S(1)} %add.163) | copy-start | bytes 1572868
  266.5 11.4 %collective-permute-start.2 = (f32[8,128,128]{2,1,0:T(8,128)S(1)}, f32[8,128,128]{2,1,0:T(8,128)S(1)}, u32[]{:S(2)}, u32[]{:S(2)}) collective-permute-start(f32[8,128,128]{2,1,0:T(8,128)S(1)} %bitcast.111), channel_id=1, source_target_pairs={{0,4},{4,8},{8,12},{12,16},{16,20},{20,24},{24,28},{1,5},{5,9},{9,... | collective-permute-start | bytes 1572872 | tf_op jit(solution)/shard_map/ppermute | solution.py:31
Sparse Core Ops, SparseCore 0:
  11.0 54.4 all-reduce.5
  191.3 25.8 all-gather.1
where the time goes:
time: 288 us; the launch traced here: 286 us
  local copies, waits for them, and re-layouts  79.5 us (28%)
  waiting for transfers between devices  66.1 us (23%)
  starting transfers between devices  46.1 us (16%)
  other arithmetic  40.4 us (14%)
  matrix products  38 us (13%)
  between operations  14.3 us (5%)
    mul x12, other arithmetic, advance(): open_cells * (current + strength * diffusivity * laplace - 0.5 * transport)  35.6 us
    ppermute x12, waiting for transfers between devices, padded(): lax.ppermute(lax.slice_in_dim(block, 0, width, axis=dim), axis, backward)  30.8 us
    ppermute x12, starting transfers between devices, padded(): lax.ppermute(lax.slice_in_dim(block, block.shape[dim] - width, None, axis...  28.3 us
    all_gather x1, waiting for transfers between devices, on_device(): every_jump = lax.all_gather(coarse_jump, 'tm', axis=0, tiled=True)  26 us
    dot_general x10, matrix products, apply_coarse(): jnp.einsum('...tik,tlk->...til', mixed_x, matrix_y, precision=exact_preci...  24.6 us
    ppermute x12, starting transfers between devices, padded(): lax.ppermute(lax.slice_in_dim(block, 0, width, axis=dim), axis, backward)  15.5 us
    dot_general x10, matrix products, apply_coarse(): jnp.einsum('tij,...tjk->...tik', matrix_x, coarse_values, precision=exact...  13.5 us
    dynamic_update_slice x8, local copies, waits for them, and re-layouts, on_device(): last_state, history = lax.scan(sweep, first_coarse, every_jump)  13.4 us
  transfers between devices with their start and end apart: 27, of which 14 were waited for; matrix products, arithmetic and copies ran while one was open for 37% of the time, Pallas kernels for 0%

commit v1 on v0

--- a/solution.py
+++ b/solution.py
@@ -81,7 +81,16 @@
     correction = fine_ends - prolong(apply_coarse(restrict(starts), coarse_x, coarse_y))
     coarse_jump = restrict(correction)
     first_coarse = spread(restrict(starts[0]), "tm", 0)
-    every_jump = lax.all_gather(coarse_jump, "tm", axis=0, tiled=True)
+    ways = lax.axis_size("tm")
+    up = [(d, (d + 1) % ways) for d in range(ways)]
+    down = [(d, (d - 1) % ways) for d in range(ways)]
+    earlier, later = ([coarse_jump], [coarse_jump])
+    for _ in range(ways // 2):
+        earlier.append(lax.ppermute(earlier[-1], "tm", up))
+    for _ in range((ways - 1) // 2):
+        later.append(lax.ppermute(later[-1], "tm", down))
+    line = jnp.concatenate([*earlier[::-1], *later[1:]], axis=0)
+    every_jump = jnp.roll(line, (lax.axis_index("tm") - ways // 2) * coarse_jump.shape[0], axis=0)
 
     def sweep(state_now, jump):
         return (apply_coarse(state_now, coarse_x, coarse_y) + jump, state_now)

time: 288 us -> 335 us (1.16)
  starting transfers between devices: 46.1 us -> 80.1 us
  waiting for transfers between devices: 66.1 us -> 81.4 us
  matrix products: 38 us -> 31.2 us
  local copies, waits for them, and re-layouts: 79.5 us -> 83.2 us
    psum x1, waiting for transfers between devices: 0.02 us -> 48.4 us  [spread(): return lax.psum(kept, axis)]
    ppermute x12, waiting for transfers between devices: 30.8 us -> 0.03 us  [padded(): lax.ppermute(lax.slice_in_dim(block, 0, width, axis=dim), axis, backward)]
    ppermute x12, starting transfers between devices: 28.3 us -> 54.6 us  [padded(): lax.ppermute(lax.slice_in_dim(block, block.shape[dim] - width, None, axis...]
    all_gather x1 -> x0, waiting for transfers between devices: 26 us -> none  [on_device(): every_jump = lax.all_gather(coarse_jump, 'tm', axis=0, tiled=True)]
    ppermute x0 -> x7, waiting for transfers between devices: none -> 23.5 us  [the longest x4 23.5 us: on_device(): earlier.append(lax.ppermute(earlier[-1], 'tm', up))]
    ppermute x0 -> x7, starting transfers between devices: none -> 8.04 us  [the longest x3 7.98 us: on_device(): later.append(lax.ppermute(later[-1], 'tm', down))]
    dot_general x10, matrix products: 24.6 us -> 17.8 us  [apply_coarse(): jnp.einsum('...tik,tlk->...til', mixed_x, matrix_y, precision=exact_preci...]
  transfers between devices with their start and end apart: 27 -> 33, of which waited for: 14 -> 6; matrix products, arithmetic and copies ran while one was open for 37% -> 7% of each run, Pallas kernels for 0% -> 0%
where the time goes in v1:
time: 335 us; the launch traced here: 333 us
  local copies, waits for them, and re-layouts  83.2 us (25%)
  waiting for transfers between devices  81.4 us (24%)
  starting transfers between devices  80.1 us (24%)
  other arithmetic  41.1 us (12%)
  matrix products  31.2 us (9%)
  between operations  14.5 us (4%)
    ppermute x12, starting transfers between devices, padded(): lax.ppermute(lax.slice_in_dim(block, block.shape[dim] - width, None, axis...  54.6 us
    psum x1, waiting for transfers between devices, spread(): return lax.psum(kept, axis)  48.4 us
    mul x12, other arithmetic, advance(): open_cells * (current + strength * diffusivity * laplace - 0.5 * transport)  35 us
    ppermute x4, waiting for transfers between devices, on_device(): earlier.append(lax.ppermute(earlier[-1], 'tm', up))  23.5 us
    dot_general x10, matrix products, apply_coarse(): jnp.einsum('...tik,tlk->...til', mixed_x, matrix_y, precision=exact_preci...  17.8 us
    ppermute x12, starting transfers between devices, padded(): lax.ppermute(lax.slice_in_dim(block, 0, width, axis=dim), axis, backward)  15.5 us
    dynamic_update_slice x8, local copies, waits for them, and re-layouts, on_device(): last_state, history = lax.scan(sweep, first_coarse, every_jump)  13.4 us
    dot_general x10, matrix products, apply_coarse(): jnp.einsum('tij,...tjk->...tik', matrix_x, coarse_values, precision=exact...  13.3 us
  transfers between devices with their start and end apart: 33, of which 6 were waited for; matrix products, arithmetic and copies ran while one was open for 7% of the time, Pallas kernels for 0%

profile of v1, /device:TPU:4, one launch (start us, length us, event | category | flops | bytes accessed | tf_op | source)
XLA Modules:
  0.0 332.6 jit_solution(1930930146000571336)
XLA Ops:
  7.2 1.4 copy.17
  8.6 1.7 slice.112
  10.3 1.7 slice.113
  17.4 166.1 %while.25 = (s32[]{:T(128)}, f32[1,8,128,128]{2,1,3,0:T(8,128)S(1)}, f32[8,128,128]{1,0,2:T(8,128)}, f32[12]{0:T(128)S(1)}, f32[8,128,128]{1,0,2:T(8,128)}, /*in...) while((s32[]{:T(128)}, ...), condition=%wide.region_2.3_spmd, body=%wide.region_1.2_spmd.sunk | while | flops 2710714 | bytes 10800029 | solution.py:80
  19.0 4.5 %collective-permute-start.1 = (f32[1,8,4,128]{3,2,1,0:T(4,128)S(1)}, f32[1,8,4,128]{3,2,1,0:T(4,128)S(1)}, u32[]{:S(2)}, u32[]{:S(2)}) collective-permute-start(f32[1,8,4,128]{3,2,1,0:T(4,128)S(1)} %pad_maximum_fusion.6), channel_id=1, source_target_pairs={{0,1},{1,2},{2,3},{4,5},{5,6},{6,7},{8,9},{9,10},{10,11},{12,13},{... | collective-permute-start | bytes 49160 | tf_op jit(solution)/shard_map/while/body/eval_jaxpr/ppermute | solution.py:15
  28.3 2.9 fusion.60
  32.8 4.5 %collective-permute-start.1 = (f32[1,8,4,128]{3,2,1,0:T(4,128)S(1)}, f32[1,8,4,128]{3,2,1,0:T(4,128)S(1)}, u32[]{:S(2)}, u32[]{:S(2)}) collective-permute-start(f32[1,8,4,128]{3,2,1,0:T(4,128)S(1)} %pad_maximum_fusion.6), channel_id=1, source_target_pairs={{0,1},{1,2},{2,3},{4,5},{5,6},{6,7},{8,9},{9,10},{10,11},{12,13},{... | collective-permute-start | bytes 49160 | tf_op jit(solution)/shard_map/while/body/eval_jaxpr/ppermute | solution.py:15
  42.1 2.9 fusion.60
  46.7 4.5 %collective-permute-start.1 = (f32[1,8,4,128]{3,2,1,0:T(4,128)S(1)}, f32[1,8,4,128]{3,2,1,0:T(4,128)S(1)}, u32[]{:S(2)}, u32[]{:S(2)}) collective-permute-start(f32[1,8,4,128]{3,2,1,0:T(4,128)S(1)} %pad_maximum_fusion.6), channel_id=1, source_target_pairs={{0,1},{1,2},{2,3},{4,5},{5,6},{6,7},{8,9},{9,10},{10,11},{12,13},{... | collective-permute-start | bytes 49160 | tf_op jit(solution)/shard_map/while/body/eval_jaxpr/ppermute | solution.py:15
  56.0 2.9 fusion.60
  60.5 4.5 %collective-permute-start.1 = (f32[1,8,4,128]{3,2,1,0:T(4,128)S(1)}, f32[1,8,4,128]{3,2,1,0:T(4,128)S(1)}, u32[]{:S(2)}, u32[]{:S(2)}) collective-permute-start(f32[1,8,4,128]{3,2,1,0:T(4,128)S(1)} %pad_maximum_fusion.6), channel_id=1, source_target_pairs={{0,1},{1,2},{2,3},{4,5},{5,6},{6,7},{8,9},{9,10},{10,11},{12,13},{... | collective-permute-start | bytes 49160 | tf_op jit(solution)/shard_map/while/body/eval_jaxpr/ppermute | solution.py:15
  69.8 2.9 fusion.60
  74.3 4.5 %collective-permute-start.1 = (f32[1,8,4,128]{3,2,1,0:T(4,128)S(1)}, f32[1,8,4,128]{3,2,1,0:T(4,128)S(1)}, u32[]{:S(2)}, u32[]{:S(2)}) collective-permute-start(f32[1,8,4,128]{3,2,1,0:T(4,128)S(1)} %pad_maximum_fusion.6), channel_id=1, source_target_pairs={{0,1},{1,2},{2,3},{4,5},{5,6},{6,7},{8,9},{9,10},{10,11},{12,13},{... | collective-permute-start | bytes 49160 | tf_op jit(solution)/shard_map/while/body/eval_jaxpr/ppermute | solution.py:15
  83.7 2.9 fusion.60
  88.2 4.5 %collective-permute-start.1 = (f32[1,8,4,128]{3,2,1,0:T(4,128)S(1)}, f32[1,8,4,128]{3,2,1,0:T(4,128)S(1)}, u32[]{:S(2)}, u32[]{:S(2)}) collective-permute-start(f32[1,8,4,128]{3,2,1,0:T(4,128)S(1)} %pad_maximum_fusion.6), channel_id=1, source_target_pairs={{0,1},{1,2},{2,3},{4,5},{5,6},{6,7},{8,9},{9,10},{10,11},{12,13},{... | collective-permute-start | bytes 49160 | tf_op jit(solution)/shard_map/while/body/eval_jaxpr/ppermute | solution.py:15
  97.5 2.9 fusion.60
  102.0 4.5 %collective-permute-start.1 = (f32[1,8,4,128]{3,2,1,0:T(4,128)S(1)}, f32[1,8,4,128]{3,2,1,0:T(4,128)S(1)}, u32[]{:S(2)}, u32[]{:S(2)}) collective-permute-start(f32[1,8,4,128]{3,2,1,0:T(4,128)S(1)} %pad_maximum_fusion.6), channel_id=1, source_target_pairs={{0,1},{1,2},{2,3},{4,5},{5,6},{6,7},{8,9},{9,10},{10,11},{12,13},{... | collective-permute-start | bytes 49160 | tf_op jit(solution)/shard_map/while/body/eval_jaxpr/ppermute | solution.py:15
  111.3 2.9 fusion.60
  115.9 4.5 %collective-permute-start.1 = (f32[1,8,4,128]{3,2,1,0:T(4,128)S(1)}, f32[1,8,4,128]{3,2,1,0:T(4,128)S(1)}, u32[]{:S(2)}, u32[]{:S(2)}) collective-permute-start(f32[1,8,4,128]{3,2,1,0:T(4,128)S(1)} %pad_maximum_fusion.6), channel_id=1, source_target_pairs={{0,1},{1,2},{2,3},{4,5},{5,6},{6,7},{8,9},{9,10},{10,11},{12,13},{... | collective-permute-start | bytes 49160 | tf_op jit(solution)/shard_map/while/body/eval_jaxpr/ppermute | solution.py:15
  125.2 2.9 fusion.60
  129.7 4.5 %collective-permute-start.1 = (f32[1,8,4,128]{3,2,1,0:T(4,128)S(1)}, f32[1,8,4,128]{3,2,1,0:T(4,128)S(1)}, u32[]{:S(2)}, u32[]{:S(2)}) collective-permute-start(f32[1,8,4,128]{3,2,1,0:T(4,128)S(1)} %pad_maximum_fusion.6), channel_id=1, source_target_pairs={{0,1},{1,2},{2,3},{4,5},{5,6},{6,7},{8,9},{9,10},{10,11},{12,13},{... | collective-permute-start | bytes 49160 | tf_op jit(solution)/shard_map/while/body/eval_jaxpr/ppermute | solution.py:15
  139.0 2.9 fusion.60
  143.5 4.5 %collective-permute-start.1 = (f32[1,8,4,128]{3,2,1,0:T(4,128)S(1)}, f32[1,8,4,128]{3,2,1,0:T(4,128)S(1)}, u32[]{:S(2)}, u32[]{:S(2)}) collective-permute-start(f32[1,8,4,128]{3,2,1,0:T(4,128)S(1)} %pad_maximum_fusion.6), channel_id=1, source_target_pairs={{0,1},{1,2},{2,3},{4,5},{5,6},{6,7},{8,9},{9,10},{10,11},{12,13},{... | collective-permute-start | bytes 49160 | tf_op jit(solution)/shard_map/while/body/eval_jaxpr/ppermute | solution.py:15
  152.9 2.9 fusion.60
  157.4 4.5 %collective-permute-start.1 = (f32[1,8,4,128]{3,2,1,0:T(4,128)S(1)}, f32[1,8,4,128]{3,2,1,0:T(4,128)S(1)}, u32[]{:S(2)}, u32[]{:S(2)}) collective-permute-start(f32[1,8,4,128]{3,2,1,0:T(4,128)S(1)} %pad_maximum_fusion.6), channel_id=1, source_target_pairs={{0,1},{1,2},{2,3},{4,5},{5,6},{6,7},{8,9},{9,10},{10,11},{12,13},{... | collective-permute-start | bytes 49160 | tf_op jit(solution)/shard_map/while/body/eval_jaxpr/ppermute | solution.py:15
  166.7 2.9 fusion.60
  171.2 4.5 %collective-permute-start.1 = (f32[1,8,4,128]{3,2,1,0:T(4,128)S(1)}, f32[1,8,4,128]{3,2,1,0:T(4,128)S(1)}, u32[]{:S(2)}, u32[]{:S(2)}) collective-permute-start(f32[1,8,4,128]{3,2,1,0:T(4,128)S(1)} %pad_maximum_fusion.6), channel_id=1, source_target_pairs={{0,1},{1,2},{2,3},{4,5},{5,6},{6,7},{8,9},{9,10},{10,11},{12,13},{... | collective-permute-start | bytes 49160 | tf_op jit(solution)/shard_map/while/body/eval_jaxpr/ppermute | solution.py:15
  180.5 2.9 fusion.60
  183.7 1.4 convolution_bitcast_fusion.1
  185.1 2.2 fusion.32
  187.9 6.7 %collective-permute-done.2 = f32[1,8,64,128]{3,2,1,0:T(8,128)S(1)} collective-permute-done((f32[1,8,64,128]{3,2,1,0:T(8,128)S(1)}, f32[1,8,64,128]{3,2,1,0:T(8,128)S(1)}, u32[]{:S(2)}, u32[]{:S(2)}) %collective-permute-start.2) | collective-permute-done | bytes 262176 | tf_op jit(solution)/shard_map/ppermute | solution.py:89
  194.6 2.6 collective-permute-start.6
  197.2 6.8 %collective-permute-done.3 = f32[1,8,64,128]{3,2,1,0:T(8,128)S(1)} collective-permute-done((f32[1,8,64,128]{3,2,1,0:T(8,128)S(1)}, f32[1,8,64,128]{3,2,1,0:T(8,128)S(1)}, u32[]{:S(2)}, u32[]{:S(2)}) %collective-permute-start.3) | collective-permute-done | bytes 262176 | tf_op jit(solution)/shard_map/ppermute | solution.py:89
  204.0 2.6 collective-permute-start.7
  206.7 5.9 %collective-permute-done.4 = f32[1,8,64,128]{3,2,1,0:T(8,128)S(1)} collective-permute-done((f32[1,8,64,128]{3,2,1,0:T(8,128)S(1)}, f32[1,8,64,128]{3,2,1,0:T(8,128)S(1)}, u32[]{:S(2)}, u32[]{:S(2)}) %collective-permute-start.4) | collective-permute-done | bytes 262176 | tf_op jit(solution)/shard_map/ppermute | solution.py:89
  213.5 1.7 multiply_select_fusion
  215.2 2.7 collective-permute-start.8
  217.9 4.1 %collective-permute-done.5 = f32[1,8,64,128]{3,2,1,0:T(8,128)S(1)} collective-permute-done((f32[1,8,64,128]{3,2,1,0:T(8,128)S(1)}, f32[1,8,64,128]{3,2,1,0:T(8,128)S(1)}, u32[]{:S(2)}, u32[]{:S(2)}) %collective-permute-start.5) | collective-permute-done | bytes 262176 | tf_op jit(solution)/shard_map/ppermute | solution.py:89
  222.8 48.4 %all-reduce.6.cloned.1.call-done = f32[8,64,128]{2,1,0:T(8,128)} async-done(((f32[8,64,128]{2,1,0:T(8,128)}), f32[8,64,128]{2,1,0:T(8,128)}) %all-reduce.6.cloned.1.call-update) | async-done | bytes 262160 | tf_op jit(solution)/shard_map/psum | solution.py:25
  271.2 38.6 %while.26 = (s32[]{:T(128)}, f32[8,64,128]{2,1,0:T(8,128)}, f32[8,8,64,128]{3,2,1,0:T(8,128)}, f32[8,64,64]{2,1,0:T(8,128)S(1)}, f32[8,128,128]{2,1,0:T(8,128)S(1)}, /*index=5*/f32[8,8,64,128]{3,2,1,0:T(8,128)S(1)}, s32[]{:T(128)}) while((s32[]{:T(128)}, f32[8,64,128]{2,1,0:T(8,128)}, f32[8,8,64,128]{3,2,1,0:T(8,128)}, ...), condition=%wide.region_4.5_spmd, body=%wide.region_3.4_spmd.sunk | while | flops 151060480 | bytes 2490961 | solution.py:98
  271.2 1.7 bitcast_dynamic-update-slice_fusion.2
  272.8 1.3 fusion.65
  274.2 1.8 convolution_add_fusion.2
  276.0 1.7 bitcast_dynamic-update-slice_fusion.2
  277.7 1.3 fusion.65
  279.0 1.8 convolution_add_fusion.2
  280.8 1.7 bitcast_dynamic-update-slice_fusion.2
  282.5 1.3 fusion.65
  283.8 1.8 convolution_add_fusion.2
  285.6 1.7 bitcast_dynamic-update-slice_fusion.2
  288.6 1.8 convolution_add_fusion.2
  290.5 1.7 bitcast_dynamic-update-slice_fusion.2
  292.1 1.3 fusion.65
  293.4 1.8 convolution_add_fusion.2
  295.3 1.7 bitcast_dynamic-update-slice_fusion.2
  296.9 1.3 fusion.65
  298.3 1.8 convolution_add_fusion.2
  300.1 1.7 bitcast_dynamic-update-slice_fusion.2
  301.8 1.3 fusion.65
  303.1 1.8 convolution_add_fusion.2
  304.9 1.7 bitcast_dynamic-update-slice_fusion.2
  307.9 1.8 convolution_add_fusion.2
  313.5 1.9 collective-permute-start.9
  315.4 9.5 %collective-permute-done.9 = f32[8,128,128]{2,1,0:T(8,128)S(1)} collective-permute-done((f32[8,128,128]{2,1,0:T(8,128)S(1)}, f32[8,128,128]{2,1,0:T(8,128)S(1)}, u32[]{:S(2)}, u32[]{:S(2)}) %collective-permute-start.9) | collective-permute-done | bytes 524320 | tf_op jit(solution)/shard_map/ppermute | solution.py:31
  (295 shorter events, 90.3 us)
Async XLA Ops:
  7.2 8.1 %copy-start.5 = (s32[8,128,128]{2,1,0:T(8,128)S(1)}, s32[8,128,128]{2,1,0:T(8,128)}, u32[]{:S(2)}) copy-start(s32[8,128,128]{2,1,0:T(8,128)} %param.15) | copy-start | bytes 1572868
  7.2 264.0 %all-reduce.6.cloned.1.call-start = ((), (), s32[]{:S(2)}) async-start(), calls=%async_computation | async-start | bytes 524288 | tf_op jit(solution)/shard_map/psum | solution.py:25
  7.2 9.1 %copy-start.6 = (f32[8,128,128]{2,1,0:T(8,128)S(1)}, f32[8,128,128]{2,1,0:T(8,128)}, u32[]{:S(2)}) copy-start(f32[8,128,128]{2,1,0:T(8,128)} %param.13) | copy-start | bytes 1572868
  8.6 8.8 %copy-start.7 = (s32[8,4]{0,1:T(4,128)S(1)}, s32[8,4]{0,1:T(4,128)}, u32[]{:S(2)}) copy-start(s32[8,4]{0,1:T(4,128)} %param.17) | copy-start | bytes 388
  8.6 8.8 %copy-start.8 = (f32[12]{0:T(128)S(1)}, f32[12]{0:T(128)}, u32[]{:S(2)}) copy-start(f32[12]{0:T(128)} %param.16) | copy-start | bytes 148
  17.4 166.3 %copy-start.1 = (f32[8,64,64]{2,1,0:T(8,128)S(1)}, f32[8,64,64]{2,1,0:T(8,128)}, u32[]{:S(2)}) copy-start(f32[8,64,64]{2,1,0:T(8,128)} %param.18) | copy-start | bytes 393220
  17.7 7.6 %collective-permute-start = (f32[1,8,4,128]{3,2,1,0:T(4,128)S(1)}, f32[1,8,4,128]{3,2,1,0:T(4,128)S(1)}, u32[]{:S(2)}, u32[]{:S(2)}) collective-permute-start(f32[1,8,4,128]{3,2,1,0:T(4,128)S(1)} %pad_maximum_fusion.6), channel_id=1, source_target_pairs={{1,0},{2,1},{3,2},{5,4},{6,5},{7,6},{9,8},{10,9},{11,10},{13,12},{... | collective-permute-start | bytes 49160 | tf_op jit(solution)/shard_map/while/body/eval_jaxpr/ppermute | solution.py:18
  19.0 6.3 %collective-permute-start.1 = (f32[1,8,4,128]{3,2,1,0:T(4,128)S(1)}, f32[1,8,4,128]{3,2,1,0:T(4,128)S(1)}, u32[]{:S(2)}, u32[]{:S(2)}) collective-permute-start(f32[1,8,4,128]{3,2,1,0:T(4,128)S(1)} %pad_maximum_fusion.6), channel_id=1, source_target_pairs={{0,1},{1,2},{2,3},{4,5},{5,6},{6,7},{8,9},{9,10},{10,11},{12,13},{... | collective-permute-start | bytes 49160 | tf_op jit(solution)/shard_map/while/body/eval_jaxpr/ppermute | solution.py:15
  31.5 7.6 %collective-permute-start = (f32[1,8,4,128]{3,2,1,0:T(4,128)S(1)}, f32[1,8,4,128]{3,2,1,0:T(4,128)S(1)}, u32[]{:S(2)}, u32[]{:S(2)}) collective-permute-start(f32[1,8,4,128]{3,2,1,0:T(4,128)S(1)} %pad_maximum_fusion.6), channel_id=1, source_target_pairs={{1,0},{2,1},{3,2},{5,4},{6,5},{7,6},{9,8},{10,9},{11,10},{13,12},{... | collective-permute-start | bytes 49160 | tf_op jit(solution)/shard_map/while/body/eval_jaxpr/ppermute | solution.py:18
  32.8 6.3 %collective-permute-start.1 = (f32[1,8,4,128]{3,2,1,0:T(4,128)S(1)}, f32[1,8,4,128]{3,2,1,0:T(4,128)S(1)}, u32[]{:S(2)}, u32[]{:S(2)}) collective-permute-start(f32[1,8,4,128]{3,2,1,0:T(4,128)S(1)} %pad_maximum_fusion.6), channel_id=1, source_target_pairs={{0,1},{1,2},{2,3},{4,5},{5,6},{6,7},{8,9},{9,10},{10,11},{12,13},{... | collective-permute-start | bytes 49160 | tf_op jit(solution)/shard_map/while/body/eval_jaxpr/ppermute | solution.py:15
  45.4 7.6 %collective-permute-start = (f32[1,8,4,128]{3,2,1,0:T(4,128)S(1)}, f32[1,8,4,128]{3,2,1,0:T(4,128)S(1)}, u32[]{:S(2)}, u32[]{:S(2)}) collective-permute-start(f32[1,8,4,128]{3,2,1,0:T(4,128)S(1)} %pad_maximum_fusion.6), channel_id=1, source_target_pairs={{1,0},{2,1},{3,2},{5,4},{6,5},{7,6},{9,8},{10,9},{11,10},{13,12},{... | collective-permute-start | bytes 49160 | tf_op jit(solution)/shard_map/while/body/eval_jaxpr/ppermute | solution.py:18
  46.7 6.3 %collective-permute-start.1 = (f32[1,8,4,128]{3,2,1,0:T(4,128)S(1)}, f32[1,8,4,128]{3,2,1,0:T(4,128)S(1)}, u32[]{:S(2)}, u32[]{:S(2)}) collective-permute-start(f32[1,8,4,128]{3,2,1,0:T(4,128)S(1)} %pad_maximum_fusion.6), channel_id=1, source_target_pairs={{0,1},{1,2},{2,3},{4,5},{5,6},{6,7},{8,9},{9,10},{10,11},{12,13},{... | collective-permute-start | bytes 49160 | tf_op jit(solution)/shard_map/while/body/eval_jaxpr/ppermute | solution.py:15
  59.2 7.6 %collective-permute-start = (f32[1,8,4,128]{3,2,1,0:T(4,128)S(1)}, f32[1,8,4,128]{3,2,1,0:T(4,128)S(1)}, u32[]{:S(2)}, u32[]{:S(2)}) collective-permute-start(f32[1,8,4,128]{3,2,1,0:T(4,128)S(1)} %pad_maximum_fusion.6), channel_id=1, source_target_pairs={{1,0},{2,1},{3,2},{5,4},{6,5},{7,6},{9,8},{10,9},{11,10},{13,12},{... | collective-permute-start | bytes 49160 | tf_op jit(solution)/shard_map/while/body/eval_jaxpr/ppermute | solution.py:18
  60.5 6.3 %collective-permute-start.1 = (f32[1,8,4,128]{3,2,1,0:T(4,128)S(1)}, f32[1,8,4,128]{3,2,1,0:T(4,128)S(1)}, u32[]{:S(2)}, u32[]{:S(2)}) collective-permute-start(f32[1,8,4,128]{3,2,1,0:T(4,128)S(1)} %pad_maximum_fusion.6), channel_id=1, source_target_pairs={{0,1},{1,2},{2,3},{4,5},{5,6},{6,7},{8,9},{9,10},{10,11},{12,13},{... | collective-permute-start | bytes 49160 | tf_op jit(solution)/shard_map/while/body/eval_jaxpr/ppermute | solution.py:15
  73.0 7.6 %collective-permute-start = (f32[1,8,4,128]{3,2,1,0:T(4,128)S(1)}, f32[1,8,4,128]{3,2,1,0:T(4,128)S(1)}, u32[]{:S(2)}, u32[]{:S(2)}) collective-permute-start(f32[1,8,4,128]{3,2,1,0:T(4,128)S(1)} %pad_maximum_fusion.6), channel_id=1, source_target_pairs={{1,0},{2,1},{3,2},{5,4},{6,5},{7,6},{9,8},{10,9},{11,10},{13,12},{... | collective-permute-start | bytes 49160 | tf_op jit(solution)/shard_map/while/body/eval_jaxpr/ppermute | solution.py:18
  74.3 6.3 %collective-permute-start.1 = (f32[1,8,4,128]{3,2,1,0:T(4,128)S(1)}, f32[1,8,4,128]{3,2,1,0:T(4,128)S(1)}, u32[]{:S(2)}, u32[]{:S(2)}) collective-permute-start(f32[1,8,4,128]{3,2,1,0:T(4,128)S(1)} %pad_maximum_fusion.6), channel_id=1, source_target_pairs={{0,1},{1,2},{2,3},{4,5},{5,6},{6,7},{8,9},{9,10},{10,11},{12,13},{... | collective-permute-start | bytes 49160 | tf_op jit(solution)/shard_map/while/body/eval_jaxpr/ppermute | solution.py:15
  86.9 7.6 %collective-permute-start = (f32[1,8,4,128]{3,2,1,0:T(4,128)S(1)}, f32[1,8,4,128]{3,2,1,0:T(4,128)S(1)}, u32[]{:S(2)}, u32[]{:S(2)}) collective-permute-start(f32[1,8,4,128]{3,2,1,0:T(4,128)S(1)} %pad_maximum_fusion.6), channel_id=1, source_target_pairs={{1,0},{2,1},{3,2},{5,4},{6,5},{7,6},{9,8},{10,9},{11,10},{13,12},{... | collective-permute-start | bytes 49160 | tf_op jit(solution)/shard_map/while/body/eval_jaxpr/ppermute | solution.py:18
  88.2 6.3 %collective-permute-start.1 = (f32[1,8,4,128]{3,2,1,0:T(4,128)S(1)}, f32[1,8,4,128]{3,2,1,0:T(4,128)S(1)}, u32[]{:S(2)}, u32[]{:S(2)}) collective-permute-start(f32[1,8,4,128]{3,2,1,0:T(4,128)S(1)} %pad_maximum_fusion.6), channel_id=1, source_target_pairs={{0,1},{1,2},{2,3},{4,5},{5,6},{6,7},{8,9},{9,10},{10,11},{12,13},{... | collective-permute-start | bytes 49160 | tf_op jit(solution)/shard_map/while/body/eval_jaxpr/ppermute | solution.py:15
  100.7 7.6 %collective-permute-start = (f32[1,8,4,128]{3,2,1,0:T(4,128)S(1)}, f32[1,8,4,128]{3,2,1,0:T(4,128)S(1)}, u32[]{:S(2)}, u32[]{:S(2)}) collective-permute-start(f32[1,8,4,128]{3,2,1,0:T(4,128)S(1)} %pad_maximum_fusion.6), channel_id=1, source_target_pairs={{1,0},{2,1},{3,2},{5,4},{6,5},{7,6},{9,8},{10,9},{11,10},{13,12},{... | collective-permute-start | bytes 49160 | tf_op jit(solution)/shard_map/while/body/eval_jaxpr/ppermute | solution.py:18
  102.0 6.3 %collective-permute-start.1 = (f32[1,8,4,128]{3,2,1,0:T(4,128)S(1)}, f32[1,8,4,128]{3,2,1,0:T(4,128)S(1)}, u32[]{:S(2)}, u32[]{:S(2)}) collective-permute-start(f32[1,8,4,128]{3,2,1,0:T(4,128)S(1)} %pad_maximum_fusion.6), channel_id=1, source_target_pairs={{0,1},{1,2},{2,3},{4,5},{5,6},{6,7},{8,9},{9,10},{10,11},{12,13},{... | collective-permute-start | bytes 49160 | tf_op jit(solution)/shard_map/while/body/eval_jaxpr/ppermute | solution.py:15
  114.6 7.6 %collective-permute-start = (f32[1,8,4,128]{3,2,1,0:T(4,128)S(1)}, f32[1,8,4,128]{3,2,1,0:T(4,128)S(1)}, u32[]{:S(2)}, u32[]{:S(2)}) collective-permute-start(f32[1,8,4,128]{3,2,1,0:T(4,128)S(1)} %pad_maximum_fusion.6), channel_id=1, source_target_pairs={{1,0},{2,1},{3,2},{5,4},{6,5},{7,6},{9,8},{10,9},{11,10},{13,12},{... | collective-permute-start | bytes 49160 | tf_op jit(solution)/shard_map/while/body/eval_jaxpr/ppermute | solution.py:18
  115.9 6.3 %collective-permute-start.1 = (f32[1,8,4,128]{3,2,1,0:T(4,128)S(1)}, f32[1,8,4,128]{3,2,1,0:T(4,128)S(1)}, u32[]{:S(2)}, u32[]{:S(2)}) collective-permute-start(f32[1,8,4,128]{3,2,1,0:T(4,128)S(1)} %pad_maximum_fusion.6), channel_id=1, source_target_pairs={{0,1},{1,2},{2,3},{4,5},{5,6},{6,7},{8,9},{9,10},{10,11},{12,13},{... | collective-permute-start | bytes 49160 | tf_op jit(solution)/shard_map/while/body/eval_jaxpr/ppermute | solution.py:15
  128.4 7.6 %collective-permute-start = (f32[1,8,4,128]{3,2,1,0:T(4,128)S(1)}, f32[1,8,4,128]{3,2,1,0:T(4,128)S(1)}, u32[]{:S(2)}, u32[]{:S(2)}) collective-permute-start(f32[1,8,4,128]{3,2,1,0:T(4,128)S(1)} %pad_maximum_fusion.6), channel_id=1, source_target_pairs={{1,0},{2,1},{3,2},{5,4},{6,5},{7,6},{9,8},{10,9},{11,10},{13,12},{... | collective-permute-start | bytes 49160 | tf_op jit(solution)/shard_map/while/body/eval_jaxpr/ppermute | solution.py:18
  129.7 6.3 %collective-permute-start.1 = (f32[1,8,4,128]{3,2,1,0:T(4,128)S(1)}, f32[1,8,4,128]{3,2,1,0:T(4,128)S(1)}, u32[]{:S(2)}, u32[]{:S(2)}) collective-permute-start(f32[1,8,4,128]{3,2,1,0:T(4,128)S(1)} %pad_maximum_fusion.6), channel_id=1, source_target_pairs={{0,1},{1,2},{2,3},{4,5},{5,6},{6,7},{8,9},{9,10},{10,11},{12,13},{... | collective-permute-start | bytes 49160 | tf_op jit(solution)/shard_map/while/body/eval_jaxpr/ppermute | solution.py:15
  142.2 7.6 %collective-permute-start = (f32[1,8,4,128]{3,2,1,0:T(4,128)S(1)}, f32[1,8,4,128]{3,2,1,0:T(4,128)S(1)}, u32[]{:S(2)}, u32[]{:S(2)}) collective-permute-start(f32[1,8,4,128]{3,2,1,0:T(4,128)S(1)} %pad_maximum_fusion.6), channel_id=1, source_target_pairs={{1,0},{2,1},{3,2},{5,4},{6,5},{7,6},{9,8},{10,9},{11,10},{13,12},{... | collective-permute-start | bytes 49160 | tf_op jit(solution)/shard_map/while/body/eval_jaxpr/ppermute | solution.py:18
  143.5 6.3 %collective-permute-start.1 = (f32[1,8,4,128]{3,2,1,0:T(4,128)S(1)}, f32[1,8,4,128]{3,2,1,0:T(4,128)S(1)}, u32[]{:S(2)}, u32[]{:S(2)}) collective-permute-start(f32[1,8,4,128]{3,2,1,0:T(4,128)S(1)} %pad_maximum_fusion.6), channel_id=1, source_target_pairs={{0,1},{1,2},{2,3},{4,5},{5,6},{6,7},{8,9},{9,10},{10,11},{12,13},{... | collective-permute-start | bytes 49160 | tf_op jit(solution)/shard_map/while/body/eval_jaxpr/ppermute | solution.py:15
  156.1 7.6 %collective-permute-start = (f32[1,8,4,128]{3,2,1,0:T(4,128)S(1)}, f32[1,8,4,128]{3,2,1,0:T(4,128)S(1)}, u32[]{:S(2)}, u32[]{:S(2)}) collective-permute-start(f32[1,8,4,128]{3,2,1,0:T(4,128)S(1)} %pad_maximum_fusion.6), channel_id=1, source_target_pairs={{1,0},{2,1},{3,2},{5,4},{6,5},{7,6},{9,8},{10,9},{11,10},{13,12},{... | collective-permute-start | bytes 49160 | tf_op jit(solution)/shard_map/while/body/eval_jaxpr/ppermute | solution.py:18
  157.4 6.3 %collective-permute-start.1 = (f32[1,8,4,128]{3,2,1,0:T(4,128)S(1)}, f32[1,8,4,128]{3,2,1,0:T(4,128)S(1)}, u32[]{:S(2)}, u32[]{:S(2)}) collective-permute-start(f32[1,8,4,128]{3,2,1,0:T(4,128)S(1)} %pad_maximum_fusion.6), channel_id=1, source_target_pairs={{0,1},{1,2},{2,3},{4,5},{5,6},{6,7},{8,9},{9,10},{10,11},{12,13},{... | collective-permute-start | bytes 49160 | tf_op jit(solution)/shard_map/while/body/eval_jaxpr/ppermute | solution.py:15
  169.9 7.6 %collective-permute-start = (f32[1,8,4,128]{3,2,1,0:T(4,128)S(1)}, f32[1,8,4,128]{3,2,1,0:T(4,128)S(1)}, u32[]{:S(2)}, u32[]{:S(2)}) collective-permute-start(f32[1,8,4,128]{3,2,1,0:T(4,128)S(1)} %pad_maximum_fusion.6), channel_id=1, source_target_pairs={{1,0},{2,1},{3,2},{5,4},{6,5},{7,6},{9,8},{10,9},{11,10},{13,12},{... | collective-permute-start | bytes 49160 | tf_op jit(solution)/shard_map/while/body/eval_jaxpr/ppermute | solution.py:18
  171.2 6.3 %collective-permute-start.1 = (f32[1,8,4,128]{3,2,1,0:T(4,128)S(1)}, f32[1,8,4,128]{3,2,1,0:T(4,128)S(1)}, u32[]{:S(2)}, u32[]{:S(2)}) collective-permute-start(f32[1,8,4,128]{3,2,1,0:T(4,128)S(1)} %pad_maximum_fusion.6), channel_id=1, source_target_pairs={{0,1},{1,2},{2,3},{4,5},{5,6},{6,7},{8,9},{9,10},{10,11},{12,13},{... | collective-permute-start | bytes 49160 | tf_op jit(solution)/shard_map/while/body/eval_jaxpr/ppermute | solution.py:15
  183.5 29.1 %copy-start.2 = (f32[1,8,128,128]{3,2,1,0:T(8,128)S(1)}, f32[1,8,128,128]{3,2,1,0:T(8,128)}, u32[]{:S(2)}) copy-start(f32[1,8,128,128]{3,2,1,0:T(8,128)} %param.12) | copy-start | bytes 1572868
  187.6 34.7 %copy-start.3 = (f32[1,8,128,128]{3,2,1,0:T(8,128)}, f32[1,8,128,128]{3,2,1,0:T(8,128)S(1)}, u32[]{:S(2)}) copy-start(f32[1,8,128,128]{3,2,1,0:T(8,128)S(1)} %sub.73) | copy-start | bytes 1572868
  187.9 6.7 %collective-permute-start.2 = (f32[1,8,64,128]{3,2,1,0:T(8,128)S(1)}, f32[1,8,64,128]{3,2,1,0:T(8,128)S(1)}, u32[]{:S(2)}, u32[]{:S(2)}) collective-permute-start(f32[1,8,64,128]{3,2,1,0:T(8,128)S(1)} %add_multiply_fusion), channel_id=1, source_target_pairs={{0,4},{4,8},{8,12},{12,16},{16,20},{20,24},{24,28},{28,0},{1,5},{5... | collective-permute-start | bytes 786440 | tf_op jit(solution)/shard_map/ppermute | solution.py:89
  194.6 9.4 %collective-permute-start.3 = (f32[1,8,64,128]{3,2,1,0:T(8,128)S(1)}, f32[1,8,64,128]{3,2,1,0:T(8,128)S(1)}, u32[]{:S(2)}, u32[]{:S(2)}) collective-permute-start(f32[1,8,64,128]{3,2,1,0:T(8,128)S(1)} %collective-permute-done.2), channel_id=1, source_target_pairs={{0,4},{4,8},{8,12},{12,16},{16,20},{20,24},{24,28},{28,0},{1,5},{5... | collective-permute-start | bytes 786440 | tf_op jit(solution)/shard_map/ppermute | solution.py:89
  194.6 9.4 %collective-permute-start.6 = (f32[1,8,64,128]{3,2,1,0:T(8,128)S(1)}, f32[1,8,64,128]{3,2,1,0:T(8,128)S(1)}, u32[]{:S(2)}, u32[]{:S(2)}) collective-permute-start(f32[1,8,64,128]{3,2,1,0:T(8,128)S(1)} %add_multiply_fusion), channel_id=1, source_target_pairs={{0,28},{4,0},{8,4},{12,8},{16,12},{20,16},{24,20},{28,24},{1,29},{... | collective-permute-start | bytes 786440 | tf_op jit(solution)/shard_map/ppermute | solution.py:91
  204.0 8.5 %collective-permute-start.4 = (f32[1,8,64,128]{3,2,1,0:T(8,128)S(1)}, f32[1,8,64,128]{3,2,1,0:T(8,128)S(1)}, u32[]{:S(2)}, u32[]{:S(2)}) collective-permute-start(f32[1,8,64,128]{3,2,1,0:T(8,128)S(1)} %collective-permute-done.3), channel_id=1, source_target_pairs={{0,4},{4,8},{8,12},{12,16},{16,20},{20,24},{24,28},{28,0},{1,5},{5... | collective-permute-start | bytes 786440 | tf_op jit(solution)/shard_map/ppermute | solution.py:89
  204.0 11.2 %collective-permute-start.7 = (f32[1,8,64,128]{3,2,1,0:T(8,128)S(1)}, f32[1,8,64,128]{3,2,1,0:T(8,128)S(1)}, u32[]{:S(2)}, u32[]{:S(2)}) collective-permute-start(f32[1,8,64,128]{3,2,1,0:T(8,128)S(1)} %collective-permute-done.6), channel_id=1, source_target_pairs={{0,28},{4,0},{8,4},{12,8},{16,12},{20,16},{24,20},{28,24},{1,29},{... | collective-permute-start | bytes 786440 | tf_op jit(solution)/shard_map/ppermute | solution.py:91
  212.6 9.5 %collective-permute-start.5 = (f32[1,8,64,128]{3,2,1,0:T(8,128)S(1)}, f32[1,8,64,128]{3,2,1,0:T(8,128)S(1)}, u32[]{:S(2)}, u32[]{:S(2)}) collective-permute-start(f32[1,8,64,128]{3,2,1,0:T(8,128)S(1)} %collective-permute-done.4), channel_id=1, source_target_pairs={{0,4},{4,8},{8,12},{12,16},{16,20},{20,24},{24,28},{28,0},{1,5},{5... | collective-permute-start | bytes 786440 | tf_op jit(solution)/shard_map/ppermute | solution.py:89
  215.2 7.0 %collective-permute-start.8 = (f32[1,8,64,128]{3,2,1,0:T(8,128)S(1)}, f32[1,8,64,128]{3,2,1,0:T(8,128)S(1)}, u32[]{:S(2)}, u32[]{:S(2)}) collective-permute-start(f32[1,8,64,128]{3,2,1,0:T(8,128)S(1)} %collective-permute-done.7), channel_id=1, source_target_pairs={{0,28},{4,0},{8,4},{12,8},{16,12},{20,16},{24,20},{28,24},{1,29},{... | collective-permute-start | bytes 786440 | tf_op jit(solution)/shard_map/ppermute | solution.py:91
  222.3 48.9 %copy-start = (f32[8,128,128]{2,1,0:T(8,128)S(1)}, f32[8,128,128]{2,1,0:T(8,128)}, u32[]{:S(2)}) copy-start(f32[8,128,128]{2,1,0:T(8,128)} %param.19) | copy-start | bytes 1572868
  313.5 12.3 %copy-start.4 = (f32[1,8,128,128]{3,2,1,0:T(8,128)}, f32[1,8,128,128]{3,2,1,0:T(8,128)S(1)}, u32[]{:S(2)}) copy-start(f32[1,8,128,128]{3,2,1,0:T(8,128)S(1)} %add.176) | copy-start | bytes 1572868
  313.5 11.4 %collective-permute-start.9 = (f32[8,128,128]{2,1,0:T(8,128)S(1)}, f32[8,128,128]{2,1,0:T(8,128)S(1)}, u32[]{:S(2)}, u32[]{:S(2)}) collective-permute-start(f32[8,128,128]{2,1,0:T(8,128)S(1)} %bitcast.111), channel_id=1, source_target_pairs={{0,4},{4,8},{8,12},{12,16},{16,20},{20,24},{24,28},{1,5},{5,9},{9,... | collective-permute-start | bytes 1572872 | tf_op jit(solution)/shard_map/ppermute | solution.py:31
Sparse Core Ops, SparseCore 0:
  215.3 55.8 all-reduce.5
